TPU v7x, 512 devices: a whole 4x8x8 slice. The times are simulated.
512 devices in a mesh: req: 128 (over y, z, core), tp: 4 (over x).
Axes of the slice: x: 4, y: 8, z: 8, core: 2. Of those that a mesh axis runs over, the one named last changes fastest.
Arguments:
- qkv_rows: bfloat16 [32768, 3, 1536], P('req', None, 'tp'), may hold values from -13 to 13
- row_request: int32 [32768], P('req'), may hold values from 0 to 127, as said below
- request_owner: int32 [128], replicated, may hold values from 0 to 127, each once
- cached_len: int32 [128], P('req'), may hold values from 0 to 1024
- page_table: int32 [128, 8], P('req'), may hold values from 0 to 7, as said below
- kv_pages: bfloat16 [1024, 2, 128, 1536], P('req', None, None, 'tp'), may hold values from -6 to 6
- residual: bfloat16 [32768, 3072], P('req', 'tp'), may hold values from -128 to 128
- out_weight: bfloat16 [1536, 3072], P('tp'), may hold values from -0.15625 to 0.15625
- norm_gain: bfloat16 [3072], P('tp'), may hold values from 0.5 to 1.5
Outputs:
- new_residual: bfloat16 [32768, 3072], P('req', 'tp')
- normed: bfloat16 [32768, 3072], P('req', 'tp')
Inputs may be any that keep to these rules, and one draw needn't show every extreme that they name: `row_request`: on every device at most 5 new tokens name the same request, and one request is named by exactly 5 tokens on every device. Half of the requests are named by exactly one token in all, and no two of those tokens lie on one device. `request_owner`: each device holds the cache of exactly one request. `page_table`: each row names every page of its device's pool once.
All inputs are finite; a program needn't handle non-finite values.
Results may differ from a plain program's by a relative error of at most 0.0093.
The roundings to bfloat16 on the way count: a program that leaves them out, or rounds other values in their place, can miss the bound.
Values may be sent and summed in bfloat16 or wider, within the bound.
No kernel may reach another device: no remote copies, remote signals or barrier semaphores. Data moves between devices by JAX's collectives and lax.ppermute only.
A program may use at most 64 MiB of HBM per device.

v0:
```python
import math
import jax
import jax.numpy as jnp
from jax import lax
from jax.sharding import PartitionSpec as P

D = 3072
HEAD_SIZE = 96
SLOT = 5
REQ = ("ry", "rz", "rc")
OUTER = 8
ROPE_BASE = 10000.0
EPS = 1e-05


def rope_tables(position):
    halves = HEAD_SIZE // 2
    inverse = ROPE_BASE ** (-2.0 * jnp.arange(halves, dtype=jnp.float32) / HEAD_SIZE)
    angles = position.astype(jnp.float32)[:, None] * inverse[None, :]
    cosine = jnp.concatenate([jnp.cos(angles), jnp.cos(angles)], axis=1)
    sine_tab = jnp.concatenate([jnp.sin(angles), jnp.sin(angles)], axis=1)
    return (cosine, sine_tab)


def rotate(field, cosine, sine_tab):
    halves = HEAD_SIZE // 2
    turned = jnp.concatenate([-field[..., halves:], field[..., :halves]], axis=-1)
    return field * cosine[:, None, :] + turned * sine_tab[:, None, :]


def attend_heads(grouped, cache_keys, cache_values, cosine, sine_tab, visible):
    score_scale = 1.0 / math.sqrt(HEAD_SIZE)
    query_rows_block = rotate(grouped[:, 0].astype(jnp.float32), cosine, sine_tab).astype(
        jnp.bfloat16
    )
    fresh_keys = rotate(grouped[:, 1].astype(jnp.float32), cosine, sine_tab).astype(jnp.bfloat16)
    gathered_keys = jnp.concatenate([cache_keys, fresh_keys], axis=0)
    gathered_values = jnp.concatenate([cache_values, grouped[:, 2]], axis=0)

    def one_head(head_parts):
        head_query, head_keys, head_values = head_parts
        logit_scores = (
            jnp.einsum("md,kd->mk", head_query, head_keys, preferred_element_type=jnp.float32)
            * score_scale
        )
        logit_scores = jnp.where(visible, logit_scores, -1e30)
        top_score = jnp.max(logit_scores, axis=1, keepdims=True)
        weight = jnp.exp(logit_scores - top_score)
        softmax_weights = (weight / jnp.sum(weight, axis=1, keepdims=True)).astype(jnp.bfloat16)
        return jnp.einsum(
            "mk,kd->md", softmax_weights, head_values, preferred_element_type=jnp.float32
        ).astype(jnp.bfloat16)

    heads_out = lax.map(
        one_head,
        (
            query_rows_block.transpose(1, 0, 2),
            gathered_keys.transpose(1, 0, 2),
            gathered_values.transpose(1, 0, 2),
        ),
    )
    return heads_out.transpose(1, 0, 2)


def two_stage_all_to_all(x):
    devices = x.shape[0]
    inner = devices // OUTER
    x = x.reshape((OUTER, inner) + x.shape[1:])
    x = lax.all_to_all(x, "ry", split_axis=0, concat_axis=0, tiled=True)
    x = lax.all_to_all(x, ("rz", "rc"), split_axis=1, concat_axis=1, tiled=True)
    return x.reshape((devices,) + x.shape[2:])


def on_device(
    qkv_rows,
    row_request,
    request_owner,
    cached_len,
    page_table,
    kv_pages,
    residual,
    out_weight,
    norm_gain,
):
    row_count = qkv_rows.shape[0]
    parts = qkv_rows.shape[1]
    head_cols = qkv_rows.shape[2]
    heads_here = head_cols // HEAD_SIZE
    devices = lax.axis_size(REQ)
    slot_cap = SLOT
    buffer_len = devices * slot_cap
    device_ids = jnp.arange(devices, dtype=jnp.int32)
    row_ids = jnp.arange(row_count, dtype=jnp.int32)
    owner_dev = request_owner[row_request]
    same_owner = owner_dev[:, None] == owner_dev[None, :]
    slot_in = jnp.sum(
        (same_owner & (row_ids[None, :] < row_ids[:, None])).astype(jnp.int32), axis=1
    )
    sends_to = owner_dev[:, None] == device_ids[None, :]
    counts = jnp.sum(sends_to.astype(jnp.int32), axis=0)
    pick = (
        sends_to[None, :, :]
        & (slot_in[None, :, None] == jnp.arange(slot_cap, dtype=jnp.int32)[:, None, None])
    ).astype(jnp.bfloat16)
    slots = jnp.einsum("jid,ipc->djpc", pick, qkv_rows, preferred_element_type=jnp.float32).astype(
        jnp.bfloat16
    )
    count_row = jnp.broadcast_to(
        counts.astype(jnp.bfloat16)[:, None, None], (devices, 1, head_cols)
    )
    outgoing = jnp.concatenate(
        [slots.reshape(devices, slot_cap * parts, head_cols), count_row], axis=1
    )
    arrived = two_stage_all_to_all(outgoing)
    arrived_counts = arrived[:, slot_cap * parts, 0].astype(jnp.int32)
    length = cached_len[0]
    pool_pages = kv_pages[page_table[0]]
    cache_span = pool_pages.shape[0] * pool_pages.shape[2]
    cache_keys = pool_pages[:, 0].reshape(cache_span, heads_here, HEAD_SIZE)
    cache_values = pool_pages[:, 1].reshape(cache_span, heads_here, HEAD_SIZE)
    live_slot = (jnp.arange(slot_cap, dtype=jnp.int32)[None, :] < arrived_counts[:, None]).reshape(
        buffer_len
    )
    live_int = live_slot.astype(jnp.int32)
    new_rank = jnp.cumsum(live_int) - live_int
    cosine, sine_tab = rope_tables(length + new_rank)
    cache_ok = jnp.broadcast_to(
        (jnp.arange(cache_span, dtype=jnp.int32) < length)[None, :], (buffer_len, cache_span)
    )
    new_ok = live_slot[None, :] & (new_rank[None, :] <= new_rank[:, None])
    visible = jnp.concatenate([cache_ok, new_ok], axis=1)
    grouped = arrived[:, : slot_cap * parts].reshape(buffer_len, parts, heads_here, HEAD_SIZE)
    result = attend_heads(grouped, cache_keys, cache_values, cosine, sine_tab, visible)
    returned = two_stage_all_to_all(result.reshape(devices, slot_cap * parts, head_cols // parts))
    target = owner_dev * slot_cap + slot_in
    attn_rows = returned.reshape(buffer_len, head_cols)[target]
    partial_sum = jnp.dot(attn_rows, out_weight, preferred_element_type=jnp.float32)
    mixed_cols = lax.psum_scatter(
        partial_sum.astype(jnp.bfloat16), "tp", scatter_dimension=1, tiled=True
    ).astype(jnp.float32)
    hidden = residual.astype(jnp.float32) + mixed_cols
    square_sum = lax.psum(jnp.sum(hidden * hidden, axis=1), "tp")
    inv_rms = lax.rsqrt(square_sum / D + EPS)
    normed = hidden * inv_rms[:, None] * norm_gain.astype(jnp.float32)[None, :]
    return (hidden.astype(jnp.bfloat16), normed.astype(jnp.bfloat16))


def solution(mesh):
    req_size = mesh.shape["req"]
    split_mesh = jax.sharding.Mesh(
        mesh.devices.reshape(OUTER, req_size // OUTER // 2, 2, mesh.shape["tp"]), REQ + ("tp",)
    )
    return jax.shard_map(
        on_device,
        mesh=split_mesh,
        in_specs=(
            P(REQ, None, "tp"),
            P(REQ),
            P(),
            P(REQ),
            P(REQ, None),
            P(REQ, None, None, "tp"),
            P(REQ, "tp"),
            P("tp", None),
            P("tp"),
        ),
        out_specs=(P(REQ, "tp"), P(REQ, "tp")),
        check_vma=False,
    )
```

profile of v0, /device:TPU:8, one launch (start us, length us, event | category | flops | bytes accessed | tf_op | source)
XLA Modules:
  0.0 255.4 jit_solution(9583415751893050044)
XLA Ops:
  7.2 0.8 compare_select_fusion.1
  8.0 1.9 gather_fusion
  9.9 0.2 convert_reduce_fusion
  10.3 1.7 convolution_convert_fusion.1
  11.9 2.0 copy.62
  14.0 0.2 broadcast_in_dim.16
  14.3 2.0 pad_maximum_fusion
  16.2 45.9 %all_to_all.20 = bf16[8,16,16,384]{3,2,1,0:T(8,128)(2,1)S(1)} all-to-all(bf16[8,16,16,384]{3,2,1,0:T(8,128)(2,1)S(1)} %pad_maximum_fusion), channel_id=1, replica_groups=mesh['ry'=8,'rz'=8,'rc'=2,'tp'=4] {'ry'}, dimensions={0} | all-to-all | bytes 3145728 | tf_op jit(solution)/shard_map/all_to_all | solution.py:69
  62.1 1.4 copy.63
  63.5 10.6 %all-to-all-start.1 = ((bf16[8,16,16,384]{3,2,0,1:T(8,128)(2,1)}), bf16[8,16,16,384]{3,2,0,1:T(8,128)(2,1)}, u32[]{:S(2)}, u32[]{:S(2)}) async-start(bf16[8,16,16,384]{3,2,0,1:T(8,128)(2,1)} %copy.63), calls=%async_computation.1 | async-start | bytes 3145728 | tf_op jit(solution)/shard_map/all_to_all | solution.py:70
  74.8 3.3 %gather_fusion.1 = bf16[8,2,128,384]{3,2,1,0:T(8,128)(2,1)} fusion(bf16[8,2,128,384]{3,2,1,0:T(8,128)(2,1)} %param.16, s32[1024]{0:T(1024)S(1)} %pad_clamp_fusion.1), kind=kCustom, calls=%fused_computation.1 | custom fusion | bytes 3145760 | tf_op jit(solution)/shard_map/gather | solution.py:117
  78.1 2.8 %fusion.31 = (bf16[8,1,128,384]{3,2,1,0:T(8,128)(2,1)}, bf16[8,1,128,384]{3,2,1,0:T(8,128)(2,1)}) fusion(bf16[8,2,128,384]{3,2,1,0:T(8,128)(2,1)} %gather_fusion.1), kind=kLoop, calls=%fused_computation.78 | loop fusion | bytes 3145728 | tf_op jit(solution)/shard_map/slice | solution.py:120
  80.9 1.6 copy.66
  82.5 1.2 reshape_squeeze.6
  83.7 1.6 copy.68
  85.3 1.2 reshape_squeeze.7
  86.6 25.4 %all-to-all-done.1 = bf16[8,16,16,384]{3,2,0,1:T(8,128)(2,1)} async-done(((bf16[8,16,16,384]{3,2,0,1:T(8,128)(2,1)}), bf16[8,16,16,384]{3,2,0,1:T(8,128)(2,1)}, u32[]{:S(2)}, u32[]{:S(2)}) %all-to-all-start.1) | async-done | bytes 1572896 | tf_op jit(solution)/shard_map/all_to_all | solution.py:70
  112.0 1.6 copy.64
  113.6 1.1 copy-done.2
  114.7 2.4 fusion.27
  117.2 0.2 reshape.235
  117.4 0.3 reduce-window.9
  117.9 0.2 lt.89
  118.1 4.9 %reshape.231 = bf16[640,3,4,96]{3,2,1,0:T(4,128)(2,1)} reshape(bf16[128,15,384]{2,1,0:T(8,128)(2,1)} %bitcast.88) | data formatting | bytes 2949120 | tf_op jit(solution)/shard_map/reshape | solution.py:132
  123.0 2.7 %slice_bitcast_fusion = (bf16[640,4,96]{2,1,0:T(4,128)(2,1)}, f32[640,4,96]{2,1,0:T(4,128)S(1)}, f32[640,4,96]{2,1,0:T(4,128)S(1)}) fusion(bf16[640,3,4,96]{3,2,1,0:T(4,128)(2,1)} %reshape.231), kind=kLoop, calls=%fused_computation.38 | loop fusion | flops 491520 | bytes 3932160 | tf_op jit(solution)/shard_map/squeeze | solution.py:38
  125.7 1.2 multiply_cosine_fusion
  126.9 0.2 pad_maximum_fusion.1
  127.2 1.5 slice_negate_fusion
  128.7 2.7 %fusion.16 = (bf16[640,4,96]{2,1,0:T(4,128)(2,1)S(1)}, bf16[4,640,96]{2,0,1:T(4,128)(2,1)}) fusion(f32[640,4,48]{2,1,0:T(4,128)S(1)} %get-tuple-element.89, f32[640,4,48]{2,1,0:T(4,128)S(1)} %get-tuple-element.88, f32[640,96]{1,0:T(8,128)S(1)} %get-tuple-element.101, f32[640,96]{1,0:T(8,128)S(1)} %get-tuple-element.100, ...), kind=kLoop, calls=%fused_computation.31 | loop fusion | flops 2949120 | bytes 4423680 | tf_op jit(solution)/shard_map/convert_element_type | solution.py:36
  131.4 1.4 copy.67
  132.8 2.1 copy.70
  134.9 1.1 compare_and_fusion
  136.0 2.1 copy.69
  138.2 2.3 maximum_bitcast_fusion
  140.5 0.4 pad_add_fusion
  140.9 1.2 maximum_bitcast_fusion.1
  142.0 22.0 %while.10 = (s32[]{:T(128)}, bf16[4,640,96]{1,2,0:T(8,128)(2,1)}, bf16[4,640,96]{2,1,0:T(8,128)(2,1)}, bf16[4,1664,96]{1,2,0:T(8,128)(2,1)}, pred[640,1664]{1,0:...) while((s32[]{:T(128)}, bf16[4,640,96]{1,2,0:T(8,128)(2,1)}, bf16[4,640,96]{2,1,0:T(8,128)(2,1)}, ...), condition=%wide.region_7.8_spmd, body=%wide.region_4.7_spmd.sunk | while | flops 417524480 | bytes 14785101 | solution.py:54
  142.0 2.1 fusion.39
  144.2 0.7 fusion.40
  144.9 2.6 %fusion.41 = bf16[4,640,96]{1,2,0:T(8,128)(2,1)} fusion(bf16[4,640,96]{1,2,0:T(8,128)(2,1)} %get-tuple-element.151, s32[]{:T(128)} %get-tuple-element.150, f32[640,1664]{1,0:T(8,128)S(1)} %get-tuple-element.141, f32[640]{0:T(1024)S(1)} %fusion.40, f32[640]{0:T(1024)S(1)} %get-tuple-element.142, bf16[4,1664,96]{1,2,0:T(8,128)(2,1)} %get-tuple-element.162), kind=kOutput, calls=%fused_computation.10.clone.1 | convolution fusion | flops 207728640 | bytes 4708352 | tf_op jit(solution)/shard_map/while/body/eval_jaxpr/mk,kd->md/dot_general | solution.py:50
  147.5 2.1 fusion.39
  149.7 0.7 fusion.40
  150.4 2.6 %fusion.41 = bf16[4,640,96]{1,2,0:T(8,128)(2,1)} fusion(bf16[4,640,96]{1,2,0:T(8,128)(2,1)} %get-tuple-element.151, s32[]{:T(128)} %get-tuple-element.150, f32[640,1664]{1,0:T(8,128)S(1)} %get-tuple-element.141, f32[640]{0:T(1024)S(1)} %fusion.40, f32[640]{0:T(1024)S(1)} %get-tuple-element.142, bf16[4,1664,96]{1,2,0:T(8,128)(2,1)} %get-tuple-element.162), kind=kOutput, calls=%fused_computation.10.clone.1 | convolution fusion | flops 207728640 | bytes 4708352 | tf_op jit(solution)/shard_map/while/body/eval_jaxpr/mk,kd->md/dot_general | solution.py:50
  153.0 2.1 fusion.39
  155.2 0.7 fusion.40
  155.9 2.6 %fusion.41 = bf16[4,640,96]{1,2,0:T(8,128)(2,1)} fusion(bf16[4,640,96]{1,2,0:T(8,128)(2,1)} %get-tuple-element.151, s32[]{:T(128)} %get-tuple-element.150, f32[640,1664]{1,0:T(8,128)S(1)} %get-tuple-element.141, f32[640]{0:T(1024)S(1)} %fusion.40, f32[640]{0:T(1024)S(1)} %get-tuple-element.142, bf16[4,1664,96]{1,2,0:T(8,128)(2,1)} %get-tuple-element.162), kind=kOutput, calls=%fused_computation.10.clone.1 | convolution fusion | flops 207728640 | bytes 4708352 | tf_op jit(solution)/shard_map/while/body/eval_jaxpr/mk,kd->md/dot_general | solution.py:50
  158.5 2.1 fusion.39
  160.7 0.7 fusion.40
  161.4 2.6 %fusion.41 = bf16[4,640,96]{1,2,0:T(8,128)(2,1)} fusion(bf16[4,640,96]{1,2,0:T(8,128)(2,1)} %get-tuple-element.151, s32[]{:T(128)} %get-tuple-element.150, f32[640,1664]{1,0:T(8,128)S(1)} %get-tuple-element.141, f32[640]{0:T(1024)S(1)} %fusion.40, f32[640]{0:T(1024)S(1)} %get-tuple-element.142, bf16[4,1664,96]{1,2,0:T(8,128)(2,1)} %get-tuple-element.162), kind=kOutput, calls=%fused_computation.10.clone.1 | convolution fusion | flops 207728640 | bytes 4708352 | tf_op jit(solution)/shard_map/while/body/eval_jaxpr/mk,kd->md/dot_general | solution.py:50
  164.0 1.7 copy.73
  165.7 0.6 reshape_reshape.6
  166.3 0.1 copy.74
  166.5 20.6 %all_to_all.21 = bf16[8,16,15,128]{3,1,2,0:T(8,128)(2,1)S(1)} all-to-all(bf16[8,16,15,128]{3,1,2,0:T(8,128)(2,1)S(1)} %copy.74), channel_id=1, replica_groups=mesh['ry'=8,'rz'=8,'rc'=2,'tp'=4] {'ry'}, dimensions={0} | all-to-all | bytes 983040 | tf_op jit(solution)/shard_map/all_to_all | solution.py:69
  187.1 0.9 copy.75
  188.0 4.0 %all-to-all-start.3 = ((bf16[8,16,15,128]{3,0,2,1:T(8,128)(2,1)}), bf16[8,16,15,128]{3,0,2,1:T(8,128)(2,1)S(1)}, u32[]{:S(2)}, u32[]{:S(2)}) async-start(bf16[8,16,15,128]{3,0,2,1:T(8,128)(2,1)} %copy.75), calls=%async_computation.3 | async-start | bytes 983040 | tf_op jit(solution)/shard_map/all_to_all | solution.py:70
  192.1 15.4 %all-to-all-done.3 = bf16[8,16,15,128]{3,0,2,1:T(8,128)(2,1)S(1)} async-done(((bf16[8,16,15,128]{3,0,2,1:T(8,128)(2,1)}), bf16[8,16,15,128]{3,0,2,1:T(8,128)(2,1)S(1)}, u32[]{:S(2)}, u32[]{:S(2)}) %all-to-all-start.3) | async-done | bytes 491552 | tf_op jit(solution)/shard_map/all_to_all | solution.py:70
  207.5 0.3 reshape_reshape.7
  207.8 1.2 gather_fusion.2
  209.0 2.1 convolution_convert_fusion
  211.1 0.7 copy-done.8
  211.8 24.5 %reduce-scatter.2.cloned.1.call-done = bf16[256,768]{1,0:T(8,128)(2,1)} async-done(((bf16[256,3072]{1,0:T(8,128)(2,1)}), bf16[256,768]{1,0:T(8,128)(2,1)}) %reduce-scatter.2.cloned.1.call-update) | async-done | bytes 393232 | tf_op jit(solution)/shard_map/reduce_scatter | solution.py:138
  236.3 1.2 multiply_reduce_fusion
  237.5 9.1 %psum.7 = f32[256]{0:T(256)S(1)} all-reduce(f32[256]{0:T(256)S(1)} %multiply_reduce_fusion), channel_id=1, replica_groups=mesh['ry'=8,'rz'=8,'rc'=2,'tp'=4] {'tp'}, use_global_device_ids=true, to_apply=%region_10.11 | all-reduce | flops 256 | bytes 2048 | tf_op jit(solution)/shard_map/psum | solution.py:142
  246.6 2.0 multiply_convert_fusion
  (43 shorter events, 0.9 us)
Async XLA Ops:
  7.2 201.8 %copy-start = (bf16[384,3072]{1,0:T(8,128)(2,1)S(1)}, bf16[384,3072]{1,0:T(8,128)(2,1)}, u32[]{:S(2)}) copy-start(bf16[384,3072]{1,0:T(8,128)(2,1)} %param.18) | copy-start | bytes 7077892
  63.5 11.3 %copy-start.9 = (s32[1,8]{1,0:T(1,128)S(1)}, s32[1,8]{1,0:T(1,128)}, u32[]{:S(2)}) copy-start(s32[1,8]{1,0:T(1,128)} %param.15) | copy-start | bytes 100
  63.5 48.5 %all-to-all-start.1 = ((bf16[8,16,16,384]{3,2,0,1:T(8,128)(2,1)}), bf16[8,16,16,384]{3,2,0,1:T(8,128)(2,1)}, u32[]{:S(2)}, u32[]{:S(2)}) async-start(bf16[8,16,16,384]{3,2,0,1:T(8,128)(2,1)} %copy.63), calls=%async_computation.1 | async-start | bytes 3145728 | tf_op jit(solution)/shard_map/all_to_all | solution.py:70
  113.6 1.1 copy-start.2
  127.2 1.5 copy-start.1
  132.8 5.3 %copy-start.4 = (bf16[1024,4,96]{0,2,1:T(8,128)(2,1)S(1)}, bf16[1024,4,96]{0,2,1:T(8,128)(2,1)}, u32[]{:S(2)}) copy-start(bf16[1024,4,96]{0,2,1:T(8,128)(2,1)} %reshape_squeeze.6) | copy-start | bytes 2359300
  138.1 2.3 copy-start.6
  138.1 2.7 %copy-start.3 = (bf16[1024,4,96]{0,2,1:T(8,128)(2,1)S(1)}, bf16[1024,4,96]{0,2,1:T(8,128)(2,1)}, u32[]{:S(2)}) copy-start(bf16[1024,4,96]{0,2,1:T(8,128)(2,1)} %reshape_squeeze.7) | copy-start | bytes 2359300
  138.1 2.7 %copy-start.5 = (bf16[640,4,96]{0,2,1:T(8,128)(2,1)S(1)}, bf16[640,4,96]{0,2,1:T(8,128)(2,1)}, u32[]{:S(2)}) copy-start(bf16[640,4,96]{0,2,1:T(8,128)(2,1)} %copy.69) | copy-start | bytes 1474564
  188.0 19.4 %all-to-all-start.3 = ((bf16[8,16,15,128]{3,0,2,1:T(8,128)(2,1)}), bf16[8,16,15,128]{3,0,2,1:T(8,128)(2,1)S(1)}, u32[]{:S(2)}, u32[]{:S(2)}) async-start(bf16[8,16,15,128]{3,0,2,1:T(8,128)(2,1)} %copy.75), calls=%async_computation.3 | async-start | bytes 983040 | tf_op jit(solution)/shard_map/all_to_all | solution.py:70
  192.0 44.3 %reduce-scatter.2.cloned.1.call-start = ((), (), s32[]{:S(2)}) async-start(), calls=%async_computation.5 | async-start | bytes 1966080 | tf_op jit(solution)/shard_map/reduce_scatter | solution.py:138
  211.1 0.7 copy-start.8
  211.1 25.2 %copy-start.7 = (bf16[256,768]{1,0:T(8,128)(2,1)S(1)}, bf16[256,768]{1,0:T(8,128)(2,1)}, u32[]{:S(2)}) copy-start(bf16[256,768]{1,0:T(8,128)(2,1)} %param.17) | copy-start | bytes 1179652
Sparse Core Ops, SparseCore 0:
  211.3 24.9 reduce-scatter.1
where the time goes:
time: 257 us; the launch traced here: 255 us
  blocking collectives  75.5 us (29%)
  waiting for transfers between devices  65.3 us (25%)
  local copies, waits for them, and re-layouts  36.8 us (14%)
  other arithmetic  25.4 us (10%)
  matrix products  22.9 us (9%)
  between operations  15 us (6%)
  starting transfers between devices  14.6 us (6%)
    all_to_all x2, blocking collectives, two_stage_all_to_all(): x = lax.all_to_all(x, 'ry', split_axis=0, concat_axis=0, tiled=True)  66.4 us
    all_to_all x2, waiting for transfers between devices, two_stage_all_to_all(): x = lax.all_to_all(x, ('rz', 'rc'), split_axis=1, concat_axis=1, tiled=True)  40.8 us
    reduce_scatter x1, waiting for transfers between devices, on_device(): lax.psum_scatter(partial_sum.astype(jnp.bfloat16), 'tp', scatter_dimensio...  24.5 us
    all_to_all x2, starting transfers between devices, two_stage_all_to_all(): x = lax.all_to_all(x, ('rz', 'rc'), split_axis=1, concat_axis=1, tiled=True)  14.6 us
    dot_general x4, matrix products, one_head(): jnp.einsum('mk,kd->md', softmax_weights, head_values, preferred_element_t...  10.6 us
    psum x1, blocking collectives, on_device(): square_sum = lax.psum(jnp.sum(hidden * hidden, axis=1), 'tp')  9.06 us
    dot_general x4, matrix products, one_head(): jnp.einsum('md,kd->mk', head_query, head_keys, preferred_element_type=jnp...  8.57 us
  transfers between devices with their start and end apart: 3, of which 3 were waited for; matrix products, arithmetic and copies ran while one was open for 5% of the time, Pallas kernels for 0%

commit v1 on v0

--- a/solution.py
+++ b/solution.py
@@ -139,7 +139,7 @@
         partial_sum.astype(jnp.bfloat16), "tp", scatter_dimension=1, tiled=True
     ).astype(jnp.float32)
     hidden = residual.astype(jnp.float32) + mixed_cols
-    square_sum = lax.psum(jnp.sum(hidden * hidden, axis=1), "tp")
+    square_sum = jnp.sum(lax.all_gather(jnp.sum(hidden * hidden, axis=1), "tp"), axis=0)
     inv_rms = lax.rsqrt(square_sum / D + EPS)
     normed = hidden * inv_rms[:, None] * norm_gain.astype(jnp.float32)[None, :]
     return (hidden.astype(jnp.bfloat16), normed.astype(jnp.bfloat16))

time: 257 us -> 256 us (level)
    psum x1 -> x0, blocking collectives: 9.06 us -> none  [on_device(): square_sum = lax.psum(jnp.sum(hidden * hidden, axis=1), 'tp')]
    all_gather x0 -> x1, blocking collectives: none -> 8.3 us  [on_device(): lax.all_gather(jnp.sum(hidden * hidden, axis=1), 'tp')]
where the time goes in v1:
time: 256 us; the launch traced here: 255 us
  blocking collectives  74.7 us (29%)
  waiting for transfers between devices  65.3 us (26%)
  local copies, waits for them, and re-layouts  36.8 us (14%)
  other arithmetic  25.4 us (10%)
  matrix products  22.9 us (9%)
  between operations  15 us (6%)
  starting transfers between devices  14.6 us (6%)
    all_to_all x2, blocking collectives, two_stage_all_to_all(): x = lax.all_to_all(x, 'ry', split_axis=0, concat_axis=0, tiled=True)  66.4 us
    all_to_all x2, waiting for transfers between devices, two_stage_all_to_all(): x = lax.all_to_all(x, ('rz', 'rc'), split_axis=1, concat_axis=1, tiled=True)  40.8 us
    reduce_scatter x1, waiting for transfers between devices, on_device(): lax.psum_scatter(partial_sum.astype(jnp.bfloat16), 'tp', scatter_dimensio...  24.5 us
    all_to_all x2, starting transfers between devices, two_stage_all_to_all(): x = lax.all_to_all(x, ('rz', 'rc'), split_axis=1, concat_axis=1, tiled=True)  14.6 us
    dot_general x4, matrix products, one_head(): jnp.einsum('mk,kd->md', softmax_weights, head_values, preferred_element_t...  10.6 us
    dot_general x4, matrix products, one_head(): jnp.einsum('md,kd->mk', head_query, head_keys, preferred_element_type=jnp...  8.57 us
    all_gather x1, blocking collectives, on_device(): lax.all_gather(jnp.sum(hidden * hidden, axis=1), 'tp')  8.3 us
  transfers between devices with their start and end apart: 3, of which 3 were waited for; matrix products, arithmetic and copies ran while one was open for 5% of the time, Pallas kernels for 0%

profile of v1, /device:TPU:8, one launch (start us, length us, event | category | flops | bytes accessed | tf_op | source)
XLA Modules:
  0.0 254.7 jit_solution(7145584580966698751)
XLA Ops:
  7.2 0.8 compare_select_fusion.1
  8.0 1.9 gather_fusion
  9.9 0.2 convert_reduce_fusion
  10.3 1.7 convolution_convert_fusion.1
  11.9 2.0 copy.62
  14.0 0.2 broadcast_in_dim.16
  14.3 2.0 pad_maximum_fusion
  16.2 45.9 %all_to_all.20 = bf16[8,16,16,384]{3,2,1,0:T(8,128)(2,1)S(1)} all-to-all(bf16[8,16,16,384]{3,2,1,0:T(8,128)(2,1)S(1)} %pad_maximum_fusion), channel_id=1, replica_groups=mesh['ry'=8,'rz'=8,'rc'=2,'tp'=4] {'ry'}, dimensions={0} | all-to-all | bytes 3145728 | tf_op jit(solution)/shard_map/all_to_all | solution.py:69
  62.1 1.4 copy.63
  63.5 10.6 %all-to-all-start.1 = ((bf16[8,16,16,384]{3,2,0,1:T(8,128)(2,1)}), bf16[8,16,16,384]{3,2,0,1:T(8,128)(2,1)}, u32[]{:S(2)}, u32[]{:S(2)}) async-start(bf16[8,16,16,384]{3,2,0,1:T(8,128)(2,1)} %copy.63), calls=%async_computation.1 | async-start | bytes 3145728 | tf_op jit(solution)/shard_map/all_to_all | solution.py:70
  74.8 3.3 %gather_fusion.1 = bf16[8,2,128,384]{3,2,1,0:T(8,128)(2,1)} fusion(bf16[8,2,128,384]{3,2,1,0:T(8,128)(2,1)} %param.16, s32[1024]{0:T(1024)S(1)} %pad_clamp_fusion.1), kind=kCustom, calls=%fused_computation.1 | custom fusion | bytes 3145760 | tf_op jit(solution)/shard_map/gather | solution.py:117
  78.1 2.8 %fusion.31 = (bf16[8,1,128,384]{3,2,1,0:T(8,128)(2,1)}, bf16[8,1,128,384]{3,2,1,0:T(8,128)(2,1)}) fusion(bf16[8,2,128,384]{3,2,1,0:T(8,128)(2,1)} %gather_fusion.1), kind=kLoop, calls=%fused_computation.78 | loop fusion | bytes 3145728 | tf_op jit(solution)/shard_map/slice | solution.py:120
  80.9 1.6 copy.66
  82.5 1.2 reshape_squeeze.6
  83.7 1.6 copy.68
  85.3 1.2 reshape_squeeze.7
  86.6 25.4 %all-to-all-done.1 = bf16[8,16,16,384]{3,2,0,1:T(8,128)(2,1)} async-done(((bf16[8,16,16,384]{3,2,0,1:T(8,128)(2,1)}), bf16[8,16,16,384]{3,2,0,1:T(8,128)(2,1)}, u32[]{:S(2)}, u32[]{:S(2)}) %all-to-all-start.1) | async-done | bytes 1572896 | tf_op jit(solution)/shard_map/all_to_all | solution.py:70
  112.0 1.6 copy.64
  113.6 1.1 copy-done.2
  114.7 2.4 fusion.27
  117.2 0.2 reshape.239
  117.4 0.3 reduce-window.9
  117.9 0.2 lt.89
  118.1 4.9 %reshape.235 = bf16[640,3,4,96]{3,2,1,0:T(4,128)(2,1)} reshape(bf16[128,15,384]{2,1,0:T(8,128)(2,1)} %bitcast.89) | data formatting | bytes 2949120 | tf_op jit(solution)/shard_map/reshape | solution.py:132
  123.0 2.7 %slice_bitcast_fusion = (bf16[640,4,96]{2,1,0:T(4,128)(2,1)}, f32[640,4,96]{2,1,0:T(4,128)S(1)}, f32[640,4,96]{2,1,0:T(4,128)S(1)}) fusion(bf16[640,3,4,96]{3,2,1,0:T(4,128)(2,1)} %reshape.235), kind=kLoop, calls=%fused_computation.38 | loop fusion | flops 491520 | bytes 3932160 | tf_op jit(solution)/shard_map/squeeze | solution.py:38
  125.7 1.2 multiply_cosine_fusion
  126.9 0.2 pad_maximum_fusion.1
  127.2 1.5 slice_negate_fusion
  128.7 2.7 %fusion.16 = (bf16[640,4,96]{2,1,0:T(4,128)(2,1)S(1)}, bf16[4,640,96]{2,0,1:T(4,128)(2,1)}) fusion(f32[640,4,48]{2,1,0:T(4,128)S(1)} %get-tuple-element.89, f32[640,4,48]{2,1,0:T(4,128)S(1)} %get-tuple-element.88, f32[640,96]{1,0:T(8,128)S(1)} %get-tuple-element.101, f32[640,96]{1,0:T(8,128)S(1)} %get-tuple-element.100, ...), kind=kLoop, calls=%fused_computation.31 | loop fusion | flops 2949120 | bytes 4423680 | tf_op jit(solution)/shard_map/convert_element_type | solution.py:36
  131.4 1.4 copy.67
  132.8 2.1 copy.70
  134.9 1.1 compare_and_fusion
  136.0 2.1 copy.69
  138.2 2.3 maximum_bitcast_fusion
  140.5 0.4 pad_add_fusion
  140.9 1.2 maximum_bitcast_fusion.1
  142.0 22.0 %while.10 = (s32[]{:T(128)}, bf16[4,640,96]{1,2,0:T(8,128)(2,1)}, bf16[4,640,96]{2,1,0:T(8,128)(2,1)}, bf16[4,1664,96]{1,2,0:T(8,128)(2,1)}, pred[640,1664]{1,0:...) while((s32[]{:T(128)}, bf16[4,640,96]{1,2,0:T(8,128)(2,1)}, bf16[4,640,96]{2,1,0:T(8,128)(2,1)}, ...), condition=%wide.region_7.8_spmd, body=%wide.region_4.7_spmd.sunk | while | flops 417524480 | bytes 14785101 | solution.py:54
  142.0 2.1 fusion.39
  144.2 0.7 fusion.40
  144.9 2.6 %fusion.41 = bf16[4,640,96]{1,2,0:T(8,128)(2,1)} fusion(bf16[4,640,96]{1,2,0:T(8,128)(2,1)} %get-tuple-element.151, s32[]{:T(128)} %get-tuple-element.150, f32[640,1664]{1,0:T(8,128)S(1)} %get-tuple-element.141, f32[640]{0:T(1024)S(1)} %fusion.40, f32[640]{0:T(1024)S(1)} %get-tuple-element.142, bf16[4,1664,96]{1,2,0:T(8,128)(2,1)} %get-tuple-element.162), kind=kOutput, calls=%fused_computation.10.clone.1 | convolution fusion | flops 207728640 | bytes 4708352 | tf_op jit(solution)/shard_map/while/body/eval_jaxpr/mk,kd->md/dot_general | solution.py:50
  147.5 2.1 fusion.39
  149.7 0.7 fusion.40
  150.4 2.6 %fusion.41 = bf16[4,640,96]{1,2,0:T(8,128)(2,1)} fusion(bf16[4,640,96]{1,2,0:T(8,128)(2,1)} %get-tuple-element.151, s32[]{:T(128)} %get-tuple-element.150, f32[640,1664]{1,0:T(8,128)S(1)} %get-tuple-element.141, f32[640]{0:T(1024)S(1)} %fusion.40, f32[640]{0:T(1024)S(1)} %get-tuple-element.142, bf16[4,1664,96]{1,2,0:T(8,128)(2,1)} %get-tuple-element.162), kind=kOutput, calls=%fused_computation.10.clone.1 | convolution fusion | flops 207728640 | bytes 4708352 | tf_op jit(solution)/shard_map/while/body/eval_jaxpr/mk,kd->md/dot_general | solution.py:50
  153.0 2.1 fusion.39
  155.2 0.7 fusion.40
  155.9 2.6 %fusion.41 = bf16[4,640,96]{1,2,0:T(8,128)(2,1)} fusion(bf16[4,640,96]{1,2,0:T(8,128)(2,1)} %get-tuple-element.151, s32[]{:T(128)} %get-tuple-element.150, f32[640,1664]{1,0:T(8,128)S(1)} %get-tuple-element.141, f32[640]{0:T(1024)S(1)} %fusion.40, f32[640]{0:T(1024)S(1)} %get-tuple-element.142, bf16[4,1664,96]{1,2,0:T(8,128)(2,1)} %get-tuple-element.162), kind=kOutput, calls=%fused_computation.10.clone.1 | convolution fusion | flops 207728640 | bytes 4708352 | tf_op jit(solution)/shard_map/while/body/eval_jaxpr/mk,kd->md/dot_general | solution.py:50
  158.5 2.1 fusion.39
  160.7 0.7 fusion.40
  161.4 2.6 %fusion.41 = bf16[4,640,96]{1,2,0:T(8,128)(2,1)} fusion(bf16[4,640,96]{1,2,0:T(8,128)(2,1)} %get-tuple-element.151, s32[]{:T(128)} %get-tuple-element.150, f32[640,1664]{1,0:T(8,128)S(1)} %get-tuple-element.141, f32[640]{0:T(1024)S(1)} %fusion.40, f32[640]{0:T(1024)S(1)} %get-tuple-element.142, bf16[4,1664,96]{1,2,0:T(8,128)(2,1)} %get-tuple-element.162), kind=kOutput, calls=%fused_computation.10.clone.1 | convolution fusion | flops 207728640 | bytes 4708352 | tf_op jit(solution)/shard_map/while/body/eval_jaxpr/mk,kd->md/dot_general | solution.py:50
  164.0 1.7 copy.73
  165.7 0.6 reshape_reshape.6
  166.3 0.1 copy.74
  166.5 20.6 %all_to_all.21 = bf16[8,16,15,128]{3,1,2,0:T(8,128)(2,1)S(1)} all-to-all(bf16[8,16,15,128]{3,1,2,0:T(8,128)(2,1)S(1)} %copy.74), channel_id=1, replica_groups=mesh['ry'=8,'rz'=8,'rc'=2,'tp'=4] {'ry'}, dimensions={0} | all-to-all | bytes 983040 | tf_op jit(solution)/shard_map/all_to_all | solution.py:69
  187.1 0.9 copy.75
  188.0 4.0 %all-to-all-start.3 = ((bf16[8,16,15,128]{3,0,2,1:T(8,128)(2,1)}), bf16[8,16,15,128]{3,0,2,1:T(8,128)(2,1)S(1)}, u32[]{:S(2)}, u32[]{:S(2)}) async-start(bf16[8,16,15,128]{3,0,2,1:T(8,128)(2,1)} %copy.75), calls=%async_computation.3 | async-start | bytes 983040 | tf_op jit(solution)/shard_map/all_to_all | solution.py:70
  192.1 15.4 %all-to-all-done.3 = bf16[8,16,15,128]{3,0,2,1:T(8,128)(2,1)S(1)} async-done(((bf16[8,16,15,128]{3,0,2,1:T(8,128)(2,1)}), bf16[8,16,15,128]{3,0,2,1:T(8,128)(2,1)S(1)}, u32[]{:S(2)}, u32[]{:S(2)}) %all-to-all-start.3) | async-done | bytes 491552 | tf_op jit(solution)/shard_map/all_to_all | solution.py:70
  207.5 0.3 reshape_reshape.7
  207.8 1.2 gather_fusion.2
  209.0 2.1 convolution_convert_fusion
  211.1 0.7 copy-done.8
  211.8 24.5 %reduce-scatter.2.cloned.1.call-done = bf16[256,768]{1,0:T(8,128)(2,1)} async-done(((bf16[256,3072]{1,0:T(8,128)(2,1)}), bf16[256,768]{1,0:T(8,128)(2,1)}) %reduce-scatter.2.cloned.1.call-update) | async-done | bytes 393232 | tf_op jit(solution)/shard_map/reduce_scatter | solution.py:138
  236.3 1.2 multiply_reduce_fusion
  237.5 8.3 %all-gather.1 = f32[4,1,256]{2,1,0:T(1,128)S(1)} all-gather(f32[1,1,256]{2,1,0:T(1,128)S(1)} %bitcast.91), channel_id=2, replica_groups=mesh['ry'=8,'rz'=8,'rc'=2,'tp'=4] {'tp'}, dimensions={0}, use_global_device_ids=true | all-gather | bytes 5120 | tf_op jit(solution)/shard_map/all_gather | solution.py:142
  245.8 2.0 multiply_convert_fusion
  (44 shorter events, 0.9 us)
Async XLA Ops:
  7.2 201.8 %copy-start = (bf16[384,3072]{1,0:T(8,128)(2,1)S(1)}, bf16[384,3072]{1,0:T(8,128)(2,1)}, u32[]{:S(2)}) copy-start(bf16[384,3072]{1,0:T(8,128)(2,1)} %param.18) | copy-start | bytes 7077892
  63.5 11.3 %copy-start.9 = (s32[1,8]{1,0:T(1,128)S(1)}, s32[1,8]{1,0:T(1,128)}, u32[]{:S(2)}) copy-start(s32[1,8]{1,0:T(1,128)} %param.15) | copy-start | bytes 100
  63.5 48.5 %all-to-all-start.1 = ((bf16[8,16,16,384]{3,2,0,1:T(8,128)(2,1)}), bf16[8,16,16,384]{3,2,0,1:T(8,128)(2,1)}, u32[]{:S(2)}, u32[]{:S(2)}) async-start(bf16[8,16,16,384]{3,2,0,1:T(8,128)(2,1)} %copy.63), calls=%async_computation.1 | async-start | bytes 3145728 | tf_op jit(solution)/shard_map/all_to_all | solution.py:70
  113.6 1.1 copy-start.2
  127.2 1.5 copy-start.1
  132.8 5.3 %copy-start.4 = (bf16[1024,4,96]{0,2,1:T(8,128)(2,1)S(1)}, bf16[1024,4,96]{0,2,1:T(8,128)(2,1)}, u32[]{:S(2)}) copy-start(bf16[1024,4,96]{0,2,1:T(8,128)(2,1)} %reshape_squeeze.6) | copy-start | bytes 2359300
  138.1 2.3 copy-start.6
  138.1 2.7 %copy-start.3 = (bf16[1024,4,96]{0,2,1:T(8,128)(2,1)S(1)}, bf16[1024,4,96]{0,2,1:T(8,128)(2,1)}, u32[]{:S(2)}) copy-start(bf16[1024,4,96]{0,2,1:T(8,128)(2,1)} %reshape_squeeze.7) | copy-start | bytes 2359300
  138.1 2.7 %copy-start.5 = (bf16[640,4,96]{0,2,1:T(8,128)(2,1)S(1)}, bf16[640,4,96]{0,2,1:T(8,128)(2,1)}, u32[]{:S(2)}) copy-start(bf16[640,4,96]{0,2,1:T(8,128)(2,1)} %copy.69) | copy-start | bytes 1474564
  188.0 19.4 %all-to-all-start.3 = ((bf16[8,16,15,128]{3,0,2,1:T(8,128)(2,1)}), bf16[8,16,15,128]{3,0,2,1:T(8,128)(2,1)S(1)}, u32[]{:S(2)}, u32[]{:S(2)}) async-start(bf16[8,16,15,128]{3,0,2,1:T(8,128)(2,1)} %copy.75), calls=%async_computation.3 | async-start | bytes 983040 | tf_op jit(solution)/shard_map/all_to_all | solution.py:70
  192.0 44.3 %reduce-scatter.2.cloned.1.call-start = ((), (), s32[]{:S(2)}) async-start(), calls=%async_computation.5 | async-start | bytes 1966080 | tf_op jit(solution)/shard_map/reduce_scatter | solution.py:138
  211.1 0.7 copy-start.8
  211.1 25.2 %copy-start.7 = (bf16[256,768]{1,0:T(8,128)(2,1)S(1)}, bf16[256,768]{1,0:T(8,128)(2,1)}, u32[]{:S(2)}) copy-start(bf16[256,768]{1,0:T(8,128)(2,1)} %param.17) | copy-start | bytes 1179652
Sparse Core Ops, SparseCore 0:
  211.3 24.9 reduce-scatter.1
